TPU v7x, 32 devices: a whole 2x2x4 slice. The times are simulated.
32 devices in a mesh: groups: 2 (over y), row: 8 (over z, x), col: 2 (over core).
Axes of the slice: x: 2, y: 2, z: 4, core: 2. Of those that a mesh axis runs over, the one named last changes fastest.
Arguments:
- tokens: bfloat16 [4, 1024, 3584], P('groups', 'row', 'col'), parts along dimension 0, may hold values from -40 to 40
- gain: float32 [3584], replicated, may hold values from 0.5 to 2
- w_query: bfloat16 [3584, 1792], P('row', 'col'), may hold values from -0.125 to 0.125
- b_query: float32 [1792], P('col'), may hold values from -24 to 24
- key_weight: bfloat16 [3584, 256], P('row', 'col'), may hold values from -0.125 to 0.125
- b_key: float32 [256], P('col'), may hold values from -24 to 24
- value_weight: bfloat16 [3584, 256], P('row', 'col'), may hold values from -0.09375 to 0.09375
- value_bias: float32 [256], P('col'), may hold values from -3 to 3
- random_block_index: int32 [4, 16, 14, 2], P('groups'), parts along dimension 0, may hold values from 0 to 15, as said below
- global_block_index: int32 [4, 2, 2], P('groups'), parts along dimension 0, may hold values from 0 to 15
Outputs:
- context: bfloat16 [4, 1024, 1792], P('groups', 'row', 'col'), parts along dimension 0
There are 2 independent parts, one for each index of `groups`. A program takes and returns all parts, laid end to end along the dimension named above; an argument that names none is the same for every part. Nothing has to cross between parts.
Inputs may be any that keep to these rules, and one draw needn't show every extreme that they name: `random_block_index`: A request group is the 56 entries of both passages whose query block lies in one aligned run of 2 blocks and whose head lies in one aligned run of 7 heads. In every request group at most 7 entries name blocks of any one aligned run of 2 blocks, and some run is named exactly 7 times.
All inputs are finite; a program needn't handle non-finite values.
Results may differ from a plain program's by a relative error of at most 0.003.
The roundings to bfloat16 on the way count: a program that leaves them out, or rounds other values in their place, can miss the bound.
Values may be sent and summed in bfloat16 or wider, within the bound.
No kernel may reach another device: no remote copies, remote signals or barrier semaphores. Data moves between devices by JAX's collectives and lax.ppermute only.
A program may use at most 128 MiB of HBM per device.

v0:
```python
import math
import jax
import jax.numpy as jnp
from jax import lax
from jax.sharding import PartitionSpec as P

HEAD_SIZE = 128
BLOCK_TOKENS = 64
RANDOM_BLOCKS = 2
GLOBAL_BLOCKS = 2
rope_base = 1000000.0
norm_eps = 1e-06


def broadcast(block, axis, source):
    block = jnp.where(lax.axis_index(axis) == source, block, jnp.zeros_like(block))
    return lax.psum(block, axis)


def padded_2(shard, sides, width):
    for axis, dim in sides:
        count, length = (lax.axis_size(axis), shard.shape[dim])
        up = [(i, (i + 1) % count) for i in range(count - 1)]
        down = [(j, i) for i, j in up]
        last = lax.slice_in_dim(shard, length - width, length, axis=dim)
        leading = lax.slice_in_dim(shard, 0, width, axis=dim)
        before = lax.ppermute(last, axis, up)
        after = lax.ppermute(leading, axis, down)
        shard = jnp.concatenate([before, shard, after], axis=dim)
    return shard


def apply_rotation(values, token_positions):
    half = values.shape[-1] // 2
    freqs = 1.0 / rope_base ** (jnp.arange(half, dtype=jnp.float32) * 2.0 / values.shape[-1])
    angles = token_positions[:, None] * freqs[None, :]
    cosine = jnp.concatenate([jnp.cos(angles), jnp.cos(angles)], axis=-1)[None, :, None, :]
    sine = jnp.concatenate([jnp.sin(angles), jnp.sin(angles)], axis=-1)[None, :, None, :]
    turned = jnp.concatenate([-values[..., half:], values[..., :half]], axis=-1)
    return values * cosine + turned * sine


def shards(
    tokens,
    gain,
    w_query,
    b_query,
    key_weight,
    b_key,
    value_weight,
    value_bias,
    random_block_index,
    global_block_index,
):
    row_count = lax.axis_size("row")
    here = lax.axis_index("row")
    column = lax.axis_index("col")
    passages, length, _ = tokens.shape
    heads_here = w_query.shape[1] // HEAD_SIZE
    pairs_here = key_weight.shape[1] // HEAD_SIZE
    passage_groups = heads_here // pairs_here
    per_device = length // BLOCK_TOKENS
    scale = 1.0 / math.sqrt(HEAD_SIZE)
    whole = lax.all_gather(tokens, "col", axis=2, tiled=True)
    widened = whole.astype(jnp.float32)
    power = jnp.mean(widened * widened, axis=-1, keepdims=True)
    normed = (
        (widened * lax.rsqrt(power + norm_eps) * gain)
        .astype(jnp.bfloat16)
        .reshape(passages * length, -1)
    )
    token_positions = (here * length + jnp.arange(length, dtype=jnp.int32)).astype(jnp.float32)

    def project(panel):
        return jnp.dot(normed, panel, preferred_element_type=jnp.float32)

    def broadcast_global(own, entry, passage_index, local_head):
        owner = entry // per_device
        offset = entry % per_device
        candidate = lax.dynamic_index_in_dim(
            own[passage_index, :, local_head], offset, 0, keepdims=False
        )
        return broadcast(candidate, "row", owner)

    query_panel, key_panel, value_panel = (
        lax.all_gather(w_query, "row", axis=0, tiled=True),
        lax.all_gather(key_weight, "row", axis=0, tiled=True),
        lax.all_gather(value_weight, "row", axis=0, tiled=True),
    )
    key = apply_rotation(
        (project(key_panel) + b_key).reshape(passages, length, pairs_here, HEAD_SIZE),
        token_positions,
    ).astype(jnp.bfloat16)
    value_rows = (
        (project(value_panel) + value_bias)
        .astype(jnp.bfloat16)
        .reshape(passages, length, pairs_here, HEAD_SIZE)
    )
    pairs = jnp.concatenate([key, value_rows], axis=-1)
    width = pairs_here * 2 * HEAD_SIZE
    padded = padded_2(pairs.reshape(passages, length, width), (("row", 1),), BLOCK_TOKENS)
    padded_blocks = padded.reshape(
        passages, per_device + 2, BLOCK_TOKENS, pairs_here, 2 * HEAD_SIZE
    )
    window = jnp.stack([padded_blocks[:, step : step + per_device] for step in range(3)], axis=2)
    window = window.reshape(passages, per_device, 3 * BLOCK_TOKENS, pairs_here, 2 * HEAD_SIZE)
    own = pairs.reshape(passages, per_device, BLOCK_TOKENS, pairs_here, 2 * HEAD_SIZE).transpose(
        0, 1, 3, 2, 4
    )
    global_here = lax.dynamic_slice_in_dim(global_block_index, column * pairs_here, pairs_here, 1)
    global_pairs = jnp.stack(
        [
            jnp.stack(
                [
                    jnp.stack(
                        [
                            broadcast_global(
                                own, global_here[passage_index, 0, slot], passage_index, 0
                            )
                            for slot in range(GLOBAL_BLOCKS)
                        ]
                    )
                ]
            )
            for passage_index in range(passages)
        ]
    )
    global_pairs = global_pairs.reshape(
        passages, pairs_here, GLOBAL_BLOCKS * BLOCK_TOKENS, 2 * HEAD_SIZE
    )
    selected = lax.dynamic_slice_in_dim(random_block_index, column * heads_here, heads_here, 2)
    rotation_table = selected.reshape(passages, row_count, per_device, heads_here, RANDOM_BLOCKS)
    rotation_table = rotation_table.transpose(1, 0, 2, 3, 4).reshape(row_count, -1)
    owners = rotation_table // per_device
    wanted = rotation_table.shape[1]
    capacity = (wanted + row_count - 1) // row_count
    order = jnp.arange(wanted, dtype=jnp.int32)
    earlier = order[None, :] < order[:, None]
    matches = (owners[:, :, None] == owners[:, None, :]) & earlier[None, :, :]
    rank = jnp.sum(matches, axis=2, dtype=jnp.int32)
    passage_of = order // (per_device * heads_here * RANDOM_BLOCKS)
    head_of = order // RANDOM_BLOCKS % heads_here
    source = (passage_of[None, :] * per_device + rotation_table % per_device) * pairs_here + (
        head_of // passage_groups
    )[None, :]
    slots = jnp.arange(capacity, dtype=jnp.int32)
    chosen = (owners[:, None, :] == here) & (rank[:, None, :] == slots[None, :, None])
    valid = jnp.any(chosen, axis=2)
    pick = jnp.sum(jnp.where(chosen, source[:, None, :], 0), axis=2)
    flat_blocks = own.reshape(-1, BLOCK_TOKENS, 2 * HEAD_SIZE)
    outgoing = jnp.where(valid[:, :, None, None], flat_blocks[pick], jnp.zeros((), jnp.bfloat16))
    incoming = lax.all_to_all(outgoing, "row", split_axis=0, concat_axis=0, tiled=True)
    mine_owner = lax.dynamic_index_in_dim(owners, here, 0, keepdims=False)
    mine_rank = lax.dynamic_index_in_dim(rank, here, 0, keepdims=False)
    arrived = incoming.reshape(row_count * capacity, BLOCK_TOKENS, 2 * HEAD_SIZE)[
        mine_owner * capacity + mine_rank
    ]
    arrived = arrived.reshape(
        passages,
        per_device,
        pairs_here,
        passage_groups,
        RANDOM_BLOCKS * BLOCK_TOKENS,
        2 * HEAD_SIZE,
    )
    window, global_pairs, arrived = (window, global_pairs, arrived)
    shaped = (project(query_panel) + b_query).reshape(passages, length, heads_here, HEAD_SIZE)
    query_rows = apply_rotation(shaped, token_positions).astype(jnp.bfloat16)
    query_block_rows = query_rows.reshape(
        passages, per_device, BLOCK_TOKENS, pairs_here, passage_groups, HEAD_SIZE
    )
    first = jnp.einsum(
        "sqbkgh,sqwkh->sqkgbw",
        query_block_rows,
        window[..., :HEAD_SIZE],
        preferred_element_type=jnp.float32,
    )
    second = jnp.einsum(
        "sqbkgh,skwh->sqkgbw",
        query_block_rows,
        global_pairs[..., :HEAD_SIZE],
        preferred_element_type=jnp.float32,
    )
    third = jnp.einsum(
        "sqbkgh,sqkgwh->sqkgbw",
        query_block_rows,
        arrived[..., :HEAD_SIZE],
        preferred_element_type=jnp.float32,
    )
    scores = jnp.concatenate([first, second, third], axis=-1) * scale
    nearby_blocks = (
        here * per_device
        + jnp.arange(per_device, dtype=jnp.int32)[:, None]
        + jnp.arange(3, dtype=jnp.int32)[None, :]
        - 1
    )
    inside = (nearby_blocks >= 0) & (nearby_blocks < row_count * per_device)
    mask = jnp.concatenate(
        [
            jnp.repeat(inside, BLOCK_TOKENS, axis=1),
            jnp.ones((per_device, (GLOBAL_BLOCKS + RANDOM_BLOCKS) * BLOCK_TOKENS), dtype=jnp.bool_),
        ],
        axis=1,
    )
    scores = jnp.where(mask[None, :, None, None, None, :], scores, -jnp.inf)
    top = jnp.max(scores, axis=-1, keepdims=True)
    weights = jnp.exp(scores - top)
    probs = (weights / jnp.sum(weights, axis=-1, keepdims=True)).astype(jnp.bfloat16)
    near_probs = probs[..., : 3 * BLOCK_TOKENS]
    global_probs = probs[..., 3 * BLOCK_TOKENS : (3 + GLOBAL_BLOCKS) * BLOCK_TOKENS]
    random_probs = probs[..., (3 + GLOBAL_BLOCKS) * BLOCK_TOKENS :]
    mixed = jnp.einsum(
        "sqkgbw,sqwkh->sqbkgh",
        near_probs,
        window[..., HEAD_SIZE:],
        preferred_element_type=jnp.float32,
    )
    mixed = mixed + jnp.einsum(
        "sqkgbw,skwh->sqbkgh",
        global_probs,
        global_pairs[..., HEAD_SIZE:],
        preferred_element_type=jnp.float32,
    )
    mixed = mixed + jnp.einsum(
        "sqkgbw,sqkgwh->sqbkgh",
        random_probs,
        arrived[..., HEAD_SIZE:],
        preferred_element_type=jnp.float32,
    )
    return mixed.reshape(passages, length, heads_here * HEAD_SIZE).astype(jnp.bfloat16)


def solution(mesh):
    placed = (
        P("groups", "row", "col"),
        P(),
        P("row", "col"),
        P("col"),
        P("row", "col"),
        P("col"),
        P("row", "col"),
        P("col"),
        P("groups", None, None, None),
        P("groups", None, None),
    )
    return jax.shard_map(
        shards, mesh=mesh, in_specs=placed, out_specs=P("groups", "row", "col"), check_vma=False
    )
```

profile of v0, /device:TPU:0, one launch (start us, length us, event | category | flops | bytes accessed | tf_op | source)
XLA Modules:
  0.0 309.3 jit_solution(14698062382800990715)
XLA Ops:
  6.5 0.7 all-gather.3.cloned.1.call-update
  7.3 0.0 all-reduce.4.cloned.1.call-start
  7.3 1.4 constant_dynamic-slice_fusion.5
  18.5 0.3 multiply_cosine_fusion.1
  18.8 0.1 pad_maximum_fusion.5
  19.0 36.6 %all_gather.13 = bf16[3584,128]{1,0:T(8,128)(2,1)} all-gather(bf16[448,128]{1,0:T(8,128)(2,1)} %param.14), channel_id=1, replica_groups=mesh['groups'=2,'row'=8,'col'=2] {'row'}, dimensions={0}, use_global_device_ids=true | all-gather | bytes 1032192 | tf_op jit(solution)/shard_map/all_gather | solution.py:87
  55.5 32.6 %all_gather.14 = bf16[3584,128]{1,0:T(8,128)(2,1)S(1)} all-gather(bf16[448,128]{1,0:T(8,128)(2,1)} %param.16), channel_id=1, replica_groups=mesh['groups'=2,'row'=8,'col'=2] {'row'}, dimensions={0}, use_global_device_ids=true | all-gather | bytes 1032192 | tf_op jit(solution)/shard_map/all_gather | solution.py:88
  88.1 2.0 fusion
  90.1 2.0 fusion.2
  92.2 0.6 convolution_add_fusion.2
  92.8 0.1 slice_negate_fusion
  92.9 0.6 fusion.8
  93.6 0.1 fusion.17
  93.7 0.6 dynamic-slice_select_fusion.1
  94.3 0.6 dynamic-slice_select_fusion.3
  95.0 0.0 all-gather.5.cloned.1.call-start
  95.0 0.7 all-gather.5.cloned.1.call-update
  95.8 0.1 copy.100
  95.9 0.1 copy.79
  96.0 0.1 copy.80
  96.1 0.3 convert_reduce_fusion
  96.4 0.2 fusion.29
  96.6 0.1 copy.84
  96.8 0.2 select_reduce_fusion
  97.0 0.1 copy.85
  97.1 0.1 reshape.590
  97.2 0.1 fusion.19
  97.4 2.0 gather_fusion
  99.3 3.0 broadcast_select_fusion
  102.3 5.9 %all-to-all-start = ((bf16[8,7,64,256]{3,2,1,0:T(8,128)(2,1)}), bf16[8,7,64,256]{3,2,1,0:T(8,128)(2,1)}, u32[]{:S(2)}, u32[]{:S(2)}) async-start(bf16[8,7,64,256]{3,2,1,0:T(8,128)(2,1)} %broadcast_select_fusion), calls=%async_computation | async-start | bytes 3670016 | tf_op jit(solution)/shard_map/all_to_all | solution.py:152
  108.2 0.1 compare_and_fusion
  108.2 0.1 broadcast_in_dim.30
  108.3 0.1 reshape.568
  108.5 0.3 multiply_cosine_fusion
  108.8 0.8 pad_maximum_fusion.7
  109.6 3.9 %collective-permute-start = (bf16[2,64,256]{2,1,0:T(8,128)(2,1)S(1)}, bf16[2,64,256]{2,1,0:T(8,128)(2,1)S(1)}, u32[]{:S(2)}, u32[]{:S(2)}) collective-permute-start(bf16[2,64,256]{2,1,0:T(8,128)(2,1)S(1)} %get-tuple-element.16), channel_id=1, source_target_pairs={{0,2},{2,4},{4,6},{6,8},{8,10},{10,12},{12,14},{1,3},{3,5},{5,7},{... | collective-permute-start | bytes 196616 | tf_op jit(solution)/shard_map/ppermute | solution.py:27
  113.5 1.5 collective-permute-start.1
  115.0 0.7 collective-permute-done
  115.7 5.5 %collective-permute-done.1 = bf16[2,64,256]{2,1,0:T(8,128)(2,1)S(1)} collective-permute-done((bf16[2,64,256]{2,1,0:T(8,128)(2,1)S(1)}, bf16[2,64,256]{2,1,0:T(8,128)(2,1)S(1)}, u32[]{:S(2)}, u32[]{:S(2)}) %collective-permute-start.1) | collective-permute-done | bytes 65568 | tf_op jit(solution)/shard_map/ppermute | solution.py:28
  121.2 0.8 pad_maximum_fusion
  122.0 55.7 %all-reduce.4.cloned.1.call-done = (bf16[1,64,256]{2,1,0:T(8,128)(2,1)}, bf16[1,64,256]{2,1,0:T(8,128)(2,1)}, bf16[1,64,256]{2,1,0:T(8,128)(2,1)}, bf16[1,64,256]{2,1,0:T(8,128)(2,1)}) async-done(((bf16[1,64,256]{2,1,0:T(8,128)(2,1)}, bf16[1,64,256]{2,1,0:T(8,128)(2,1)}, bf16[1,64,256]{2,1,0:T(8,128)(2,1)}, bf16[1,64,256]{2,1,0:T(8,128)(2,1)}), (bf16[1,64,256]{2,1,0:T(8,128)(2,1)}, ...) | async-done | bytes 131088 | tf_op jit(solution)/shard_map/psum | solution.py:17
  177.8 0.8 pad_maximum_fusion.9
  178.6 0.8 pad_maximum_fusion.10
  179.3 3.5 %gather_fusion.1 = bf16[56,64,256]{2,1,0:T(8,128)(2,1)} fusion(bf16[56,64,256]{2,1,0:T(8,128)(2,1)} %bitcast.44, s32[1024]{0:T(1024)S(1)} %pad_clamp_fusion), kind=kCustom, calls=%fused_computation.1 | custom fusion | bytes 3670240 | tf_op jit(solution)/shard_map/gather | solution.py:155
  182.8 97.3 %all-gather.5.cloned.1.call-done = bf16[3584,896]{1,0:T(8,128)(2,1)} async-done(((bf16[448,896]{1,0:T(8,128)(2,1)}), bf16[3584,896]{1,0:T(8,128)(2,1)}) %all-gather.5.cloned.1.call-update) | async-done | bytes 6422544 | tf_op jit(solution)/shard_map/all_gather | solution.py:86
  280.2 4.9 %convolution_add_fusion = f32[256,896]{1,0:T(8,128)S(1)} fusion(bf16[256,3584]{1,0:T(8,128)(2,1)S(1)} %bitcast.127, bf16[3584,896]{1,0:T(8,128)(2,1)} %all-gather.5.cloned.1.call-done, f32[896]{0:T(1024)S(1)} %copy-done.7), kind=kOutput, calls=%fused_computation.21 | convolution fusion | flops 1644396544 | bytes 9178624 | tf_op jit(solution)/shard_map/dot_general | solution.py:75
  285.1 0.1 reshape.609
  285.3 1.1 reshape.570
  286.4 1.3 fusion.41
  287.7 0.3 copy.98
  288.0 0.8 neg.7
  288.8 1.5 copy.94
  290.3 2.0 fusion.10
  292.3 0.7 convolution_bitcast_fusion.5
  293.0 0.4 convolution_bitcast_fusion
  293.4 0.3 convolution_bitcast_fusion.2
  293.7 1.5 fusion.11
  295.2 2.4 fusion.4
  297.6 2.4 divide_convert_fusion
  300.0 0.4 convolution_bitcast_fusion.4
  300.4 0.4 convolution_bitcast_fusion.3
  300.8 0.3 fusion.7
  301.2 0.3 copy.87
  301.5 1.3 convert_element_type.71
  (43 shorter events, 0.3 us)
Async XLA Ops:
  6.5 89.2 %copy-start = (s32[2,16,14,2]{1,3,2,0:T(2,128)S(1)}, s32[2,16,14,2]{1,3,2,0:T(2,128)}, u32[]{:S(2)}) copy-start(s32[2,16,14,2]{1,3,2,0:T(2,128)} %param.18) | copy-start | bytes 10756
  6.5 83.6 %copy-start.4 = (f32[3584]{0:T(1024)S(1)}, f32[3584]{0:T(1024)}, u32[]{:S(2)}) copy-start(f32[3584]{0:T(1024)} %param.11) | copy-start | bytes 43012
  6.5 81.5 %all-gather.3.cloned.1.call-start = ((), (), s32[]{:S(2)}) async-start(), calls=%async_computation.1 | async-start | bytes 2752512 | tf_op jit(solution)/shard_map/all_gather | solution.py:64
  7.3 170.5 %all-reduce.4.cloned.1.call-start = ((), (), s32[]{:S(2)}) async-start(), calls=%async_computation.3 | async-start | bytes 262144 | tf_op jit(solution)/shard_map/psum | solution.py:17
  18.9 73.2 %copy-start.6 = (f32[128]{0:T(128)S(1)}, f32[128]{0:T(128)}, u32[]{:S(2)}) copy-start(f32[128]{0:T(128)} %param.15) | copy-start | bytes 1540
  88.1 4.1 %copy-start.2 = (bf16[3584,128]{1,0:T(8,128)(2,1)S(1)}, bf16[3584,128]{1,0:T(8,128)(2,1)}, u32[]{:S(2)}) copy-start(bf16[3584,128]{1,0:T(8,128)(2,1)} %all_gather.13) | copy-start | bytes 2752516
  90.1 2.8 copy-start.5
  95.0 185.2 %all-gather.5.cloned.1.call-start = ((), (), s32[]{:S(2)}) async-start(), calls=%async_computation.2 | async-start | bytes 7225344 | tf_op jit(solution)/shard_map/all_gather | solution.py:86
  102.3 77.1 %all-to-all-start = ((bf16[8,7,64,256]{3,2,1,0:T(8,128)(2,1)}), bf16[8,7,64,256]{3,2,1,0:T(8,128)(2,1)}, u32[]{:S(2)}, u32[]{:S(2)}) async-start(bf16[8,7,64,256]{3,2,1,0:T(8,128)(2,1)} %broadcast_select_fusion), calls=%async_computation | async-start | bytes 3670016 | tf_op jit(solution)/shard_map/all_to_all | solution.py:152
  108.1 172.0 %copy-start.7 = (f32[896]{0:T(1024)S(1)}, f32[896]{0:T(1024)}, u32[]{:S(2)}) copy-start(f32[896]{0:T(1024)} %param.13) | copy-start | bytes 10756
  109.6 6.1 %collective-permute-start = (bf16[2,64,256]{2,1,0:T(8,128)(2,1)S(1)}, bf16[2,64,256]{2,1,0:T(8,128)(2,1)S(1)}, u32[]{:S(2)}, u32[]{:S(2)}) collective-permute-start(bf16[2,64,256]{2,1,0:T(8,128)(2,1)S(1)} %get-tuple-element.16), channel_id=1, source_target_pairs={{0,2},{2,4},{4,6},{6,8},{8,10},{10,12},{12,14},{1,3},{3,5},{5,7},{... | collective-permute-start | bytes 196616 | tf_op jit(solution)/shard_map/ppermute | solution.py:27
  113.5 7.7 %collective-permute-start.1 = (bf16[2,64,256]{2,1,0:T(8,128)(2,1)S(1)}, bf16[2,64,256]{2,1,0:T(8,128)(2,1)S(1)}, u32[]{:S(2)}, u32[]{:S(2)}) collective-permute-start(bf16[2,64,256]{2,1,0:T(8,128)(2,1)S(1)} %get-tuple-element.17), channel_id=1, source_target_pairs={{2,0},{4,2},{6,4},{8,6},{10,8},{12,10},{14,12},{3,1},{5,3},{7,5},{... | collective-permute-start | bytes 196616 | tf_op jit(solution)/shard_map/ppermute | solution.py:28
  287.7 4.6 %copy-start.1 = (bf16[56,64,256]{2,1,0:T(8,128)(2,1)S(1)}, bf16[56,64,256]{2,1,0:T(8,128)(2,1)}, u32[]{:S(2)}) copy-start(bf16[56,64,256]{2,1,0:T(8,128)(2,1)} %gather_fusion.1) | copy-start | bytes 5505028
  288.8 4.2 %copy-start.3 = (bf16[2,2,3,64,1,256]{5,3,2,1,0,4:T(8,128)(2,1)S(1)}, bf16[2,2,3,64,1,256]{5,3,2,1,0,4:T(8,128)(2,1)}, u32[]{:S(2)}) copy-start(bf16[2,2,3,64,1,256]{5,3,2,1,0,4:T(8,128)(2,1)} %pad_maximum_fusion) | copy-start | bytes 1179652
Sparse Core Ops, SparseCore 0:
  8.9 12.8 all-gather.2
  95.1 82.6 all-reduce.3
  180.2 99.9 all-gather.4
where the time goes:
time: 310 us; the launch traced here: 309 us
  waiting for transfers between devices  161 us (52%)
  blocking collectives  69.1 us (22%)
  between operations  23.3 us (8%)
  other arithmetic  22.5 us (7%)
  local copies, waits for them, and re-layouts  13.6 us (4%)
  starting transfers between devices  11.3 us (4%)
  matrix products  8.79 us (3%)
    all_gather x1, waiting for transfers between devices, shards(): lax.all_gather(w_query, 'row', axis=0, tiled=True)  97.3 us
    psum x1, waiting for transfers between devices, broadcast(): return lax.psum(block, axis)  55.7 us
    all_gather x1, blocking collectives, shards(): lax.all_gather(key_weight, 'row', axis=0, tiled=True)  36.6 us
    all_gather x1, blocking collectives, shards(): lax.all_gather(value_weight, 'row', axis=0, tiled=True)  32.6 us
  transfers between devices with their start and end apart: 6, of which 4 were waited for; matrix products, arithmetic and copies ran while one was open for 5% of the time, Pallas kernels for 0%

commit v1 on v0

--- a/solution.py
+++ b/solution.py
@@ -3,6 +3,7 @@
 import jax.numpy as jnp
 from jax import lax
 from jax.sharding import PartitionSpec as P
+from jax.lax import all_gather
 
 HEAD_SIZE = 128
 BLOCK_TOKENS = 64
@@ -12,9 +13,13 @@
 norm_eps = 1e-06
 
 
+def link_pipes(local_array, lane_axis):
+    return jnp.sum(all_gather(local_array, lane_axis), 0)
+
+
 def broadcast(block, axis, source):
     block = jnp.where(lax.axis_index(axis) == source, block, jnp.zeros_like(block))
-    return lax.psum(block, axis)
+    return link_pipes(block, axis)
 
 
 def padded_2(shard, sides, width):

time: 310 us -> 321 us (1.035)
  blocking collectives: 69.1 us -> 242 us
  waiting for transfers between devices: 161 us -> 1.42 us
    all_gather x0 -> x4, blocking collectives: none -> 168 us  [link_pipes(): return jnp.sum(all_gather(local_array, lane_axis), 0)]
    all_gather x1, waiting for transfers between devices: 97.3 us -> 0.01 us  [shards(): lax.all_gather(w_query, 'row', axis=0, tiled=True)]
    psum x1 -> x0, waiting for transfers between devices: 55.7 us -> none  [broadcast(): return lax.psum(block, axis)]
    ppermute x1, waiting for transfers between devices: 5.49 us -> 0.01 us  [padded_2(): after = lax.ppermute(leading, axis, down)]
  transfers between devices with their start and end apart: 6 -> 5, of which waited for: 4 -> 0; matrix products, arithmetic and copies ran while one was open for 5% -> 6% of each run, Pallas kernels for 0% -> 0%
where the time goes in v1:
time: 321 us; the launch traced here: 320 us
  blocking collectives  242 us (75%)
  between operations  24.2 us (8%)
  other arithmetic  19.9 us (6%)
  local copies, waits for them, and re-layouts  12.9 us (4%)
  starting transfers between devices  10.8 us (3%)
  matrix products  8.79 us (3%)
    all_gather x4, blocking collectives, link_pipes(): return jnp.sum(all_gather(local_array, lane_axis), 0)  168 us
    all_gather x1, blocking collectives, shards(): lax.all_gather(key_weight, 'row', axis=0, tiled=True)  38.3 us
    all_gather x1, blocking collectives, shards(): lax.all_gather(value_weight, 'row', axis=0, tiled=True)  35.1 us
  transfers between devices with their start and end apart: 5, of which 0 were waited for; matrix products, arithmetic and copies ran while one was open for 6% of the time, Pallas kernels for 0%

profile of v1, /device:TPU:0, one launch (start us, length us, event | category | flops | bytes accessed | tf_op | source)
XLA Modules:
  0.0 319.9 jit_solution(17991290679114975768)
XLA Ops:
  6.5 0.7 all-gather.3.cloned.1.call-update
  7.3 0.0 all-gather.5.cloned.1.call-start
  7.3 0.7 all-gather.5.cloned.1.call-update
  8.0 0.1 copy.118
  8.1 0.1 copy.97
  8.3 0.1 copy.98
  8.4 0.3 convert_reduce_fusion
  8.7 0.2 fusion.29
  8.9 0.1 copy.102
  9.1 0.2 select_reduce_fusion
  9.3 0.1 copy.103
  9.4 0.1 reshape.574
  9.5 0.3 multiply_cosine_fusion.1
  9.8 0.1 pad_maximum_fusion.5
  9.9 0.0 copy-start.6
  9.9 38.3 %all_gather.29 = bf16[3584,128]{1,0:T(8,128)(2,1)} all-gather(bf16[448,128]{1,0:T(8,128)(2,1)} %param.14), channel_id=1, replica_groups=mesh['groups'=2,'row'=8,'col'=2] {'row'}, dimensions={0}, use_global_device_ids=true | all-gather | bytes 1032192 | tf_op jit(solution)/shard_map/all_gather | solution.py:92
  48.2 35.1 %all_gather.30 = bf16[3584,128]{1,0:T(8,128)(2,1)S(1)} all-gather(bf16[448,128]{1,0:T(8,128)(2,1)} %param.16), channel_id=1, replica_groups=mesh['groups'=2,'row'=8,'col'=2] {'row'}, dimensions={0}, use_global_device_ids=true | all-gather | bytes 1032192 | tf_op jit(solution)/shard_map/all_gather | solution.py:93
  83.4 2.0 fusion
  85.4 0.0 copy-start.5
  85.4 2.0 fusion.2
  87.5 0.6 convolution_add_fusion.2
  88.1 0.1 slice_negate_fusion
  88.3 0.1 fusion.19
  88.4 0.6 fusion.8
  89.0 2.0 gather_fusion
  91.0 3.0 broadcast_select_fusion
  94.0 5.6 %all-to-all-start = ((bf16[8,7,64,256]{3,2,1,0:T(8,128)(2,1)}), bf16[8,7,64,256]{3,2,1,0:T(8,128)(2,1)}, u32[]{:S(2)}, u32[]{:S(2)}) async-start(bf16[8,7,64,256]{3,2,1,0:T(8,128)(2,1)} %broadcast_select_fusion), calls=%async_computation | async-start | bytes 3670016 | tf_op jit(solution)/shard_map/all_to_all | solution.py:157
  99.6 0.7 constant_dynamic-slice_fusion.5
  110.6 0.1 compare_and_fusion
  110.7 0.1 broadcast_in_dim.30
  110.8 0.1 reshape.556
  111.0 0.3 multiply_cosine_fusion
  111.3 0.8 pad_maximum_fusion.7
  112.0 0.1 fusion.17
  112.2 3.9 %collective-permute-start = (bf16[2,64,256]{2,1,0:T(8,128)(2,1)S(1)}, bf16[2,64,256]{2,1,0:T(8,128)(2,1)S(1)}, u32[]{:S(2)}, u32[]{:S(2)}) collective-permute-start(bf16[2,64,256]{2,1,0:T(8,128)(2,1)S(1)} %get-tuple-element.12), channel_id=1, source_target_pairs={{0,2},{2,4},{4,6},{6,8},{8,10},{10,12},{12,14},{1,3},{3,5},{5,7},{... | collective-permute-start | bytes 196616 | tf_op jit(solution)/shard_map/ppermute | solution.py:32
  116.1 1.3 collective-permute-start.1
  117.5 75.7 %all_gather.32 = bf16[8,64,256]{2,1,0:T(8,128)(2,1)S(1)} all-gather(bf16[1,64,256]{2,1,0:T(8,128)(2,1)S(1)} %get-tuple-element.20), channel_id=1, replica_groups=mesh['groups'=2,'row'=8,'col'=2] {'row'}, dimensions={0}, use_global_device_ids=true | all-gather | bytes 294912 | tf_op jit(solution)/shard_map/all_gather | solution.py:17
  193.3 30.9 %all_gather.34 = bf16[8,64,256]{2,1,0:T(8,128)(2,1)S(1)} all-gather(bf16[1,64,256]{2,1,0:T(8,128)(2,1)S(1)} %get-tuple-element.18), channel_id=1, replica_groups=mesh['groups'=2,'row'=8,'col'=2] {'row'}, dimensions={0}, use_global_device_ids=true | all-gather | bytes 294912 | tf_op jit(solution)/shard_map/all_gather | solution.py:17
  224.2 0.0 copy-start.8
  224.2 30.8 %all_gather.33 = bf16[8,64,256]{2,1,0:T(8,128)(2,1)S(1)} all-gather(bf16[1,64,256]{2,1,0:T(8,128)(2,1)S(1)} %get-tuple-element.21), channel_id=1, replica_groups=mesh['groups'=2,'row'=8,'col'=2] {'row'}, dimensions={0}, use_global_device_ids=true | all-gather | bytes 294912 | tf_op jit(solution)/shard_map/all_gather | solution.py:17
  255.1 30.9 %all_gather.35 = bf16[8,64,256]{2,1,0:T(8,128)(2,1)S(1)} all-gather(bf16[1,64,256]{2,1,0:T(8,128)(2,1)S(1)} %get-tuple-element.19), channel_id=1, replica_groups=mesh['groups'=2,'row'=8,'col'=2] {'row'}, dimensions={0}, use_global_device_ids=true | all-gather | bytes 294912 | tf_op jit(solution)/shard_map/all_gather | solution.py:17
  286.1 0.0 collective-permute-done.1
  286.2 0.8 pad_maximum_fusion
  286.9 0.0 all-to-all-done
  286.9 3.5 %gather_fusion.1 = bf16[56,64,256]{2,1,0:T(8,128)(2,1)} fusion(bf16[56,64,256]{2,1,0:T(8,128)(2,1)} %bitcast.48, s32[1024]{0:T(1024)S(1)} %pad_clamp_fusion), kind=kCustom, calls=%fused_computation.1 | custom fusion | bytes 3670240 | tf_op jit(solution)/shard_map/gather | solution.py:160
  290.4 4.9 %convolution_add_fusion = f32[256,896]{1,0:T(8,128)S(1)} fusion(bf16[256,3584]{1,0:T(8,128)(2,1)S(1)} %bitcast.131, bf16[3584,896]{1,0:T(8,128)(2,1)} %all-gather.5.cloned.1.call-done, f32[896]{0:T(1024)S(1)} %copy-done.8), kind=kOutput, calls=%fused_computation.21 | convolution fusion | flops 1644396544 | bytes 9178624 | tf_op jit(solution)/shard_map/dot_general | solution.py:80
  295.4 0.1 reshape.593
  295.5 1.2 reshape.558
  296.7 1.3 fusion.41
  298.0 0.3 copy.116
  298.3 0.8 neg.7
  299.1 1.5 copy.112
  300.6 2.0 fusion.10
  302.6 0.7 convolution_bitcast_fusion.5
  303.3 0.4 convolution_bitcast_fusion
  303.7 0.3 convolution_bitcast_fusion.2
  304.0 1.5 fusion.11
  305.5 2.4 fusion.4
  307.9 2.4 divide_convert_fusion
  310.3 0.4 convolution_bitcast_fusion.4
  310.7 0.4 convolution_bitcast_fusion.3
  311.1 0.3 fusion.7
  311.5 0.3 copy.105
  311.8 1.3 convert_element_type.79
  (50 shorter events, 0.5 us)
Async XLA Ops:
  6.5 1.5 copy-start
  6.5 78.9 %copy-start.4 = (f32[3584]{0:T(1024)S(1)}, f32[3584]{0:T(1024)}, u32[]{:S(2)}) copy-start(f32[3584]{0:T(1024)} %param.11) | copy-start | bytes 43012
  6.5 76.8 %all-gather.3.cloned.1.call-start = ((), (), s32[]{:S(2)}) async-start(), calls=%async_computation.1 | async-start | bytes 2752512 | tf_op jit(solution)/shard_map/all_gather | solution.py:69
  7.3 283.2 %all-gather.5.cloned.1.call-start = ((), (), s32[]{:S(2)}) async-start(), calls=%async_computation.2 | async-start | bytes 7225344 | tf_op jit(solution)/shard_map/all_gather | solution.py:91
  9.9 77.6 %copy-start.6 = (f32[128]{0:T(128)S(1)}, f32[128]{0:T(128)}, u32[]{:S(2)}) copy-start(f32[128]{0:T(128)} %param.15) | copy-start | bytes 1540
  83.4 4.1 %copy-start.2 = (bf16[3584,128]{1,0:T(8,128)(2,1)S(1)}, bf16[3584,128]{1,0:T(8,128)(2,1)}, u32[]{:S(2)}) copy-start(bf16[3584,128]{1,0:T(8,128)(2,1)} %all_gather.29) | copy-start | bytes 2752516
  85.4 3.0 copy-start.5
  91.0 8.6 %copy-start.7 = (s32[2,2,2]{2,1,0:T(2,128)S(1)}, s32[2,2,2]{2,1,0:T(2,128)}, u32[]{:S(2)}) copy-start(s32[2,2,2]{2,1,0:T(2,128)} %param.19) | copy-start | bytes 100
  94.0 192.9 %all-to-all-start = ((bf16[8,7,64,256]{3,2,1,0:T(8,128)(2,1)}), bf16[8,7,64,256]{3,2,1,0:T(8,128)(2,1)}, u32[]{:S(2)}, u32[]{:S(2)}) async-start(bf16[8,7,64,256]{3,2,1,0:T(8,128)(2,1)} %broadcast_select_fusion), calls=%async_computation | async-start | bytes 3670016 | tf_op jit(solution)/shard_map/all_to_all | solution.py:157
  112.2 173.9 %collective-permute-start = (bf16[2,64,256]{2,1,0:T(8,128)(2,1)S(1)}, bf16[2,64,256]{2,1,0:T(8,128)(2,1)S(1)}, u32[]{:S(2)}, u32[]{:S(2)}) collective-permute-start(bf16[2,64,256]{2,1,0:T(8,128)(2,1)S(1)} %get-tuple-element.12), channel_id=1, source_target_pairs={{0,2},{2,4},{4,6},{6,8},{8,10},{10,12},{12,14},{1,3},{3,5},{5,7},{... | collective-permute-start | bytes 196616 | tf_op jit(solution)/shard_map/ppermute | solution.py:32
  116.1 170.0 %collective-permute-start.1 = (bf16[2,64,256]{2,1,0:T(8,128)(2,1)S(1)}, bf16[2,64,256]{2,1,0:T(8,128)(2,1)S(1)}, u32[]{:S(2)}, u32[]{:S(2)}) collective-permute-start(bf16[2,64,256]{2,1,0:T(8,128)(2,1)S(1)} %get-tuple-element.13), channel_id=1, source_target_pairs={{2,0},{4,2},{6,4},{8,6},{10,8},{12,10},{14,12},{3,1},{5,3},{7,5},{... | collective-permute-start | bytes 196616 | tf_op jit(solution)/shard_map/ppermute | solution.py:33
  224.2 66.2 %copy-start.8 = (f32[896]{0:T(1024)S(1)}, f32[896]{0:T(1024)}, u32[]{:S(2)}) copy-start(f32[896]{0:T(1024)} %param.13) | copy-start | bytes 10756
  298.0 4.6 %copy-start.1 = (bf16[56,64,256]{2,1,0:T(8,128)(2,1)S(1)}, bf16[56,64,256]{2,1,0:T(8,128)(2,1)}, u32[]{:S(2)}) copy-start(bf16[56,64,256]{2,1,0:T(8,128)(2,1)} %gather_fusion.1) | copy-start | bytes 5505028
  299.1 4.2 %copy-start.3 = (bf16[2,2,3,64,1,256]{5,3,2,1,0,4:T(8,128)(2,1)S(1)}, bf16[2,2,3,64,1,256]{5,3,2,1,0,4:T(8,128)(2,1)}, u32[]{:S(2)}) copy-start(bf16[2,2,3,64,1,256]{5,3,2,1,0,4:T(8,128)(2,1)} %pad_maximum_fusion) | copy-start | bytes 1179652
Sparse Core Ops, SparseCore 0:
  8.9 12.8 all-gather.2
  24.0 145.8 all-gather.4
